TPU v7x, 32 devices: a whole 2x2x4 slice. The times are simulated.
32 devices in a mesh: chain: 2 (over x), ops: 8 (over z, y), sector: 2 (over core).
Axes of the slice: x: 2, y: 2, z: 4, core: 2. Of those that a mesh axis runs over, the one named last changes fastest.
Arguments:
- psi: bfloat16 [2, 8, 384, 384], P('chain', 'sector'), may hold values from -90 to 90
- left_ops: bfloat16 [2, 96, 8, 384, 384], P('chain', 'ops', 'sector'), may hold values from -1 to 2
- right_ops: bfloat16 [2, 96, 8, 384, 384], P('chain', 'ops', 'sector'), may hold values from -1 to 1
- basis: bfloat16 [2, 8, 384, 384], P('chain', 'sector'), may hold values from -0.3125 to 0.3125
- block_dims: int32 [2, 8], P('chain', 'sector'), may hold values from 64 to 384, as said below
Outputs:
- residual: float32 [2, 8, 384, 384], P('chain', 'sector', 'ops')
- thetas: float32 [2, 3], P('chain')
Inputs may be any that keep to these rules, and one draw needn't show every extreme that they name: `block_dims`: each is a multiple of 64; every section has a sector of exactly 384.
All inputs are finite; a program needn't handle non-finite values.
Results may differ from a plain program's by a relative error of at most 0.009.
Values may be sent and summed in bfloat16 or wider, within the bound.
No kernel may reach another device: no remote copies, remote signals or barrier semaphores. Data moves between devices by JAX's collectives and lax.ppermute only.
A program may use at most 128 MiB of HBM per device.

v0:
```python
import jax
import jax.numpy as jnp
from jax import lax
from jax.sharding import PartitionSpec as P

SECTORS = 8
ITERS = 3


def from_behind(block, axis, distance):
    devices = range(lax.axis_size(axis))
    route = [((i - distance) % len(devices), i) for i in devices]
    return lax.ppermute(block, axis, route)


def live_mask(block_dims, block_size):
    index_rows = jnp.arange(block_size, dtype=jnp.int32)
    limits = block_dims[:, :, None, None]
    inside = (index_rows[None, None, :, None] < limits) & (index_rows[None, None, None, :] < limits)
    return inside.astype(jnp.float32)


ROW_TILE = 64
LANE_TILE = 128
CLASSES = 8


def tile_counts(dims, block_size):
    rows = jnp.clip((dims + ROW_TILE - 1) // ROW_TILE, 0, block_size // ROW_TILE)
    cols = jnp.clip((dims + LANE_TILE - 1) // LANE_TILE, 0, block_size // LANE_TILE)
    return (rows, cols)


def tile_plan(dims, block_size):
    rows, cols = tile_counts(dims, block_size)
    row_ids = jnp.arange(block_size // ROW_TILE)[None, :, None]
    col_ids = jnp.arange(block_size // LANE_TILE)[None, None, :]
    needed = ((row_ids < rows[:, None, None]) & (col_ids < cols[:, None, None])).reshape(-1)
    total = needed.shape[0]
    place = jnp.cumsum(needed.astype(jnp.int32)) - 1
    ids = jnp.arange(total, dtype=jnp.int32)
    order = jnp.zeros(total, jnp.int32).at[jnp.where(needed, place, total)].set(ids, mode="drop")
    return (order, jnp.sum(needed.astype(jnp.int32)))


def size_classes(sectors, block_size):
    total = sectors * (block_size // ROW_TILE) * (block_size // LANE_TILE)
    return sorted({-(-k * total // CLASSES) for k in range(1, CLASSES + 1)})


def tile_index(order, size, block_size):
    per_row = block_size // LANE_TILE
    per_sector = block_size // ROW_TILE * per_row
    picked = order[:size]
    return (picked // per_sector, picked // per_row % (block_size // ROW_TILE), picked % per_row)


def tiled(array):
    block_size = array.shape[-1]
    return array.reshape(
        array.shape[:-2] + (block_size // ROW_TILE, ROW_TILE, block_size // LANE_TILE, LANE_TILE)
    )


def pack(array, order, size, lead):
    sector_ids, row_ids, col_ids = tile_index(order, size, array.shape[-1])
    where = (slice(None),) * lead + (sector_ids, row_ids, slice(None), col_ids, slice(None))
    return tiled(array)[where]


def unpack(packed, order, count, size, like, lead):
    sector_ids, row_ids, col_ids = tile_index(order, size, like.shape[-1])
    sector_ids = jnp.where(jnp.arange(size) < count, sector_ids, like.shape[lead])
    where = (slice(None),) * lead + (sector_ids, row_ids, slice(None), col_ids, slice(None))
    room = jnp.zeros(tiled(like).shape, packed.dtype)
    return room.at[where].set(packed, mode="drop").reshape(like.shape)


def class_index(block_dims, block_size, classes):
    every = lax.all_gather(block_dims[0], ("chain", "sector"))
    rows, cols = tile_counts(every, block_size)
    need = jnp.max(jnp.sum(rows * cols, axis=-1))
    return jnp.sum((jnp.asarray(classes, jnp.int32) < need).astype(jnp.int32))


def chain_move(env, send_order, recv_order, recv_count, choice, classes):

    def branch(size):

        def run(env, send_order, recv_order, recv_count):
            arrived = from_behind(pack(env, send_order, size, 2), "chain", 1)
            return unpack(arrived, recv_order, recv_count, size, env, 2)

        return run

    return lax.switch(choice, [branch(s) for s in classes], env, send_order, recv_order, recv_count)


def ops_sum(partial, order, count, choice, classes):

    def branch(size):

        def run(partial, order, count):
            summed = lax.psum(pack(partial, order, size, 1), "ops")
            return unpack(summed, order, count, size, partial, 1)

        return run

    return lax.switch(choice, [branch(s) for s in classes], partial, order, count)


def gather_sector(values):
    count = lax.axis_size("sector")
    slots = jnp.zeros((count, values.shape[0]), jnp.float32)
    slots = slots.at[lax.axis_index("sector")].set(values)
    return lax.psum(slots, "sector")


def quotient(vector_wide, sigma_full):
    norm_part = jnp.sum(vector_wide * vector_wide)
    corr_part = jnp.sum(vector_wide * sigma_full)
    local_theta = jnp.where(
        norm_part > 0, corr_part / jnp.where(norm_part > 0, norm_part, 1.0), 0.0
    )
    local_rest = sigma_full - local_theta * vector_wide
    rest_part = jnp.sum(local_rest * local_rest)
    cross_part = jnp.sum(vector_wide * local_rest)
    table = gather_sector(jnp.stack([norm_part, corr_part, rest_part, cross_part, local_theta]))
    norms, corrs, rests, crosses, thetas = (table[:, i] for i in range(5))
    rayleigh = jnp.sum(corrs) / jnp.sum(norms)
    shift = thetas - rayleigh
    spread = jnp.sum(rests + 2.0 * shift * crosses + shift * shift * norms)
    return (rayleigh, spread)


def on_device(psi, left_ops, right_ops, basis, block_dims):
    block_size = psi.shape[2]
    live = live_mask(block_dims, block_size)
    classes = size_classes(psi.shape[1], block_size)
    choice = class_index(block_dims, block_size, classes)
    own_order, own_count = tile_plan(block_dims[0], block_size)
    target_dims = from_behind(block_dims, "chain", -1)
    send_order, _ = tile_plan(target_dims[0], block_size)
    half_env = jnp.einsum(
        "ckqab,cqbd->ckqad", left_ops, basis, preferred_element_type=jnp.float32
    ).astype(jnp.bfloat16)
    boundary_ops = jnp.einsum(
        "cqba,ckqbd->ckqad", basis, half_env, preferred_element_type=jnp.float32
    ).astype(jnp.bfloat16)
    shifted = chain_move(boundary_ops, send_order, own_order, own_count, choice, classes)
    vector = jnp.where(live > 0, psi, jnp.zeros_like(psi))
    entry_count = float(SECTORS * block_size * block_size)
    share_rows = block_size // lax.axis_size("ops")
    row_start = lax.axis_index("ops") * share_rows
    residual = None
    quotients = []
    for iteration in range(ITERS):
        products = jnp.einsum(
            "ckqab,cqbd->ckqad", shifted, vector, preferred_element_type=jnp.float32
        ).astype(jnp.bfloat16)
        partial_sigma = jnp.einsum(
            "ckqad,ckqed->cqae", products, right_ops, preferred_element_type=jnp.float32
        )
        sigma_full = ops_sum(partial_sigma, own_order, own_count, choice, classes) * live
        vector_wide = vector.astype(jnp.float32)
        rayleigh, spread = quotient(vector_wide, sigma_full)
        quotients.append(rayleigh)
        residue = sigma_full - rayleigh * vector_wide
        if iteration + 1 < ITERS:
            vector = (residue * lax.rsqrt(spread / entry_count + 1e-06)).astype(jnp.bfloat16)
        else:
            residual = lax.dynamic_slice_in_dim(residue, row_start, share_rows, 2)
    thetas = jnp.stack(quotients).reshape(1, ITERS)
    return (residual, thetas)


def solution(mesh):
    in_specs = (
        P("chain", "sector", None, None),
        P("chain", "ops", "sector", None, None),
        P("chain", "ops", "sector", None, None),
        P("chain", "sector", None, None),
        P("chain", "sector"),
    )
    out_specs = (P("chain", "sector", "ops", None), P("chain", None))
    return jax.shard_map(
        on_device, mesh=mesh, in_specs=in_specs, out_specs=out_specs, check_vma=False
    )
```

profile of v0, /device:TPU:0, one launch (start us, length us, event | category | flops | bytes accessed | tf_op | source)
XLA Modules:
  0.0 997.5 jit_solution(8939563958995975156)
XLA Ops:
  7.2 3.0 collective-permute-start.8
  12.2 5.2 all-gather
  19.7 21.1 %convert_bitcast_fusion = bf16[1,12,4,384,384]{3,4,1,2,0:T(8,128)(2,1)} fusion(bf16[1,4,384,384]{3,2,1,0:T(8,128)(2,1)S(1)} %copy-done, bf16[1,12,4,384,384]{4,3,2,1,0:T(8,128)(2,1)} %param.45), kind=kOutput, calls=%fused_computation.911 | convolution fusion | flops 10885791744 | bytes 29491200 | tf_op jit(solution)/shard_map/cqba,ckqbd->ckqad/dot_general | solution.py:147
  45.8 438.7 %conditional.4 = (bf16[12,4,384,384]{3,2,0,1:T(8,128)(2,1)}) conditional(s32[]{:T(128)} %clamp.28, (s32[]{:T(128)}, s32[72]{0:T(128)S(1)}, bf16[1,12,4,384,384]{3,4,1,2,0:T(8,128)(2,1)}, s32[72]{0:T(128)S(1)}) %tuple.124, (s32[]{:T(128)}, s32[72]{0:T(128)S(1)}, bf16[1,12,4,384,384]{3,4,1,2,0:T(8,128)(2,1)}, ...), branch_computations={%region_8.10_spmd, %region_10.12_spmd, %region_12.14_spmd, %region... | conditional | flops 6480 | bytes 254806912 | solution.py:96
  56.0 42.8 %reshape.1812 = bf16[12,4,6,64,3,128]{3,2,5,4,0,1:T(8,128)(2,1)} reshape(bf16[1,12,4,384,384]{3,4,1,2,0:T(8,128)(2,1)} %get-tuple-element.537) | data formatting | bytes 28311552 | tf_op jit(solution)/shard_map/cond/branch_5_fun/reshape | solution.py:60
  98.8 34.4 %copy.314 = bf16[12,4,6,64,3,128]{5,3,4,2,1,0:T(8,128)(2,1)} copy(bf16[12,4,6,64,3,128]{3,2,5,4,0,1:T(8,128)(2,1)} %reshape.1812) | data formatting | bytes 28311552 | tf_op jit(solution)/shard_map/cond/branch_5_fun/reshape | solution.py:60
  133.3 12.7 %gather_fusion.5 = bf16[54,12,64,128]{3,2,1,0:T(8,128)(2,1)} fusion(bf16[12,4,6,64,3,128]{5,3,4,2,1,0:T(8,128)(2,1)} %copy.314, s32[54]{0:T(128)S(1)} %fusion.72), kind=kCustom, calls=%fused_computation.5 | custom fusion | bytes 21234312 | tf_op jit(solution)/shard_map/cond/branch_5_fun/gather | solution.py:68
  146.6 229.5 %collective-permute-done.5 = bf16[54,1,12,64,128]{4,3,2,0,1:T(8,128)(2,1)} collective-permute-done((bf16[54,1,12,64,128]{4,3,2,0,1:T(8,128)(2,1)}, bf16[54,1,12,64,128]{4,3,2,0,1:T(8,128)(2,1)}, u32[]{:S(2)}, u32[]{:S(2)}) %collective-permute-start.5) | collective-permute-done | bytes 10616864 | tf_op jit(solution)/shard_map/cond/branch_5_fun/ppermute | solution.py:13
  376.1 8.6 broadcast.2387
  384.8 29.5 %scatter_fusion.5 = bf16[12,4,6,64,3,128]{5,3,4,2,1,0:T(8,128)(2,1)} fusion(bf16[12,4,6,64,3,128]{5,3,4,2,1,0:T(8,128)(2,1)} %broadcast.2387, s32[54]{0:T(128)S(1)} %fusion.77, bf16[54,12,64,128]{3,2,1,0:T(8,128)(2,1)} %bitcast.35), kind=kCustom, calls=%fused_computation.37 | custom fusion | bytes 31851144 | tf_op jit(solution)/shard_map/cond/branch_5_fun/scatter | solution.py:76
  414.3 20.5 %copy.450 = bf16[12,4,6,64,3,128]{5,4,3,2,0,1:T(4,128)(2,1)} copy(bf16[12,4,6,64,3,128]{5,3,4,2,1,0:T(8,128)(2,1)} %scatter_fusion.5) | data formatting | bytes 28311552 | tf_op jit(solution)/shard_map/cond | solution.py:96
  434.8 35.9 %reshape.1820 = bf16[12,4,384,384]{3,2,0,1:T(8,128)(2,1)} reshape(bf16[12,4,6,64,3,128]{5,4,3,2,0,1:T(4,128)(2,1)} %copy.450) | data formatting | bytes 28311552 | tf_op jit(solution)/shard_map/cond | solution.py:96
  484.6 20.6 %fusion.415 = f32[1,4,384,384]{3,2,1,0:T(8,128)S(1)} fusion(bf16[12,4,384,384]{3,2,0,1:T(8,128)(2,1)} %get-tuple-element.547, bf16[1,4,384,384]{3,2,1,0:T(8,128)(2,1)S(1)} %copy-done.2, pred[4,384]{1,0:T(4,128)(4,1)S(1)} %copy-done.9, bf16[1,12,4,384,384]{4,3,2,1,0:T(8,128)(2,1)} %param.46), kind=kOutput, calls=%fused_computation.956 | convolution fusion | flops 10881073152 | bytes 31852032 | tf_op jit(solution)/shard_map/ckqad,ckqed->cqae/dot_general | solution.py:161
  505.3 135.6 %conditional.5 = (f32[1,4,384,384]{3,2,1,0:T(8,128)S(1)}) conditional(s32[]{:T(128)} %clamp.28, (s32[]{:T(128)}, s32[72]{0:T(128)S(1)}, f32[1,4,384,384]{3,2,1,0:T(8,128)S(1)}) %tuple.125, (s32[]{:T(128)}, s32[72]{0:T(128)S(1)}, f32[1,4,384,384]{3,2,1,0:T(8,128)S(1)}) %tuple.125, (s32[]{:T(128)}, s32[72]{0:T(128)S(1)}, ...), branch_computations={%region_24.27_spmd, %region_27.30_spmd, %region_30.33_spmd, %regio... | conditional | flops 595872 | bytes 47189432 | solution.py:109
  512.1 2.5 reshape.977
  514.6 2.2 copy.330
  516.8 2.4 gather_fusion.13
  519.8 98.0 %all-reduce.35.cloned.1.call-done = f32[54,1,64,128]{3,2,0,1:T(8,128)} async-done(((f32[54,1,64,128]{3,2,0,1:T(8,128)}), f32[54,1,64,128]{3,2,0,1:T(8,128)}) %all-reduce.35.cloned.1.call-update) | async-done | bytes 1769488 | tf_op jit(solution)/shard_map/cond/branch_5_fun/psum | solution.py:104
  618.2 7.9 scatter_fusion.13
  626.0 3.4 copy.331
  629.4 3.8 reshape.812
  646.9 2.7 stack.71
  650.3 2.5 psum.189
  658.2 20.2 %fusion.420 = f32[1,4,384,384]{3,2,1,0:T(8,128)S(1)} fusion(bf16[12,4,384,384]{3,2,0,1:T(8,128)(2,1)} %get-tuple-element.547, bf16[1,4,384,384]{3,2,1,0:T(8,128)(2,1)S(1)} %fusion.406, bf16[1,12,4,384,384]{4,3,2,1,0:T(8,128)(2,1)} %param.46), kind=kOutput, calls=%fused_computation.957 | convolution fusion | flops 10878713856 | bytes 31850496 | tf_op jit(solution)/shard_map/ckqad,ckqed->cqae/dot_general | solution.py:161
  678.4 130.4 %conditional.6 = (f32[1,4,384,384]{3,2,1,0:T(8,128)S(1)}) conditional(s32[]{:T(128)} %clamp.28, (s32[]{:T(128)}, s32[72]{0:T(128)S(1)}, f32[1,4,384,384]{3,2,1,0:T(8,128)S(1)}) %tuple.126, (s32[]{:T(128)}, s32[72]{0:T(128)S(1)}, f32[1,4,384,384]{3,2,1,0:T(8,128)S(1)}) %tuple.126, (s32[]{:T(128)}, s32[72]{0:T(128)S(1)}, ...), branch_computations={%region_57.60_spmd, %region_60.63_spmd, %region_63.66_spmd, %regio... | conditional | flops 595872 | bytes 47189432 | solution.py:109
  685.2 2.5 reshape.1041
  687.7 2.2 copy.346
  689.9 2.4 gather_fusion.21
  693.0 92.6 %all-reduce.51.cloned.1.call-done = f32[54,1,64,128]{3,2,0,1:T(8,128)} async-done(((f32[54,1,64,128]{3,2,0,1:T(8,128)}), f32[54,1,64,128]{3,2,0,1:T(8,128)}) %all-reduce.51.cloned.1.call-update) | async-done | bytes 1769488 | tf_op jit(solution)/shard_map/cond/branch_5_fun/psum | solution.py:104
  785.8 7.9 scatter_fusion.21
  793.7 3.4 copy.347
  797.1 3.8 reshape.828
  814.4 2.7 stack.77
  817.7 2.5 psum.190
  823.6 2.5 fusion.459
  826.1 20.3 %fusion.425 = f32[1,4,384,384]{3,2,1,0:T(8,128)S(1)} fusion(bf16[12,4,384,384]{3,2,0,1:T(8,128)(2,1)} %get-tuple-element.547, bf16[1,4,384,384]{3,2,1,0:T(8,128)(2,1)} %get-tuple-element.616, bf16[1,12,4,384,384]{4,3,2,1,0:T(8,128)(2,1)} %param.46), kind=kOutput, calls=%fused_computation.958 | convolution fusion | flops 10878713856 | bytes 31850496 | tf_op jit(solution)/shard_map/ckqad,ckqed->cqae/dot_general | solution.py:161
  846.4 124.8 %conditional.7 = (f32[1,4,384,384]{3,2,1,0:T(8,128)S(1)}) conditional(s32[]{:T(128)} %clamp.28, (s32[]{:T(128)}, s32[72]{0:T(128)S(1)}, f32[1,4,384,384]{3,2,1,0:T(8,128)S(1)}) %tuple.127, (s32[]{:T(128)}, s32[72]{0:T(128)S(1)}, f32[1,4,384,384]{3,2,1,0:T(8,128)S(1)}) %tuple.127, (s32[]{:T(128)}, s32[72]{0:T(128)S(1)}, ...), branch_computations={%region_89.92_spmd, %region_92.95_spmd, %region_95.98_spmd, %regio... | conditional | flops 595872 | bytes 47189432 | solution.py:109
  853.2 2.5 reshape.1105
  855.7 2.2 copy.362
  857.9 2.4 gather_fusion.29
  861.0 92.6 %all-reduce.67.cloned.1.call-done = f32[54,1,64,128]{3,2,0,1:T(8,128)} async-done(((f32[54,1,64,128]{3,2,0,1:T(8,128)}), f32[54,1,64,128]{3,2,0,1:T(8,128)}) %all-reduce.67.cloned.1.call-update) | async-done | bytes 1769488 | tf_op jit(solution)/shard_map/cond/branch_5_fun/psum | solution.py:104
  953.9 7.9 scatter_fusion.29
  961.7 3.4 copy.363
  965.1 3.8 reshape.844
  972.6 3.2 multiply_reduce_fusion.2
  977.7 2.6 multiply_reduce_fusion
  980.3 2.7 stack.83
  983.6 2.5 psum.191
  (88 shorter events, 30.7 us)
Async XLA Ops:
  7.2 12.5 %copy-start = (bf16[1,4,384,384]{3,2,1,0:T(8,128)(2,1)S(1)}, bf16[1,4,384,384]{3,2,1,0:T(8,128)(2,1)}, u32[]{:S(2)}) copy-start(bf16[1,4,384,384]{3,2,1,0:T(8,128)(2,1)} %param.47) | copy-start | bytes 3538948
  7.2 37.0 %collective-permute-start.8 = (s32[1,4]{1,0:T(1,128)}, s32[1,4]{1,0:T(1,128)S(1)}, u32[]{:S(2)}, u32[]{:S(2)}) collective-permute-start(s32[1,4]{1,0:T(1,128)} %param.48), channel_id=1, source_target_pairs={{16,0},{0,16},{17,1},{1,17},{18,2},{2,18},{19,3},{3,19},{20,4},{4,... | collective-permute-start | bytes 56 | tf_op jit(solution)/shard_map/ppermute | solution.py:13
  19.7 21.9 %copy-start.12 = (s32[8]{0:T(128)S(1)}, s32[8]{0:T(128)}, u32[]{:S(2)}) copy-start(s32[8]{0:T(128)} %constant.1748.clone) | copy-start | bytes 100
  19.7 23.8 %copy-start.11 = (s32[2]{0:T(128)S(1)}, s32[2]{0:T(128)}, u32[]{:S(2)}) copy-start(s32[2]{0:T(128)} %constant.1739.clone.1) | copy-start | bytes 28
  45.8 438.8 %copy-start.2 = (bf16[1,4,384,384]{3,2,1,0:T(8,128)(2,1)S(1)}, bf16[1,4,384,384]{3,2,1,0:T(8,128)(2,1)}, u32[]{:S(2)}) copy-start(bf16[1,4,384,384]{3,2,1,0:T(8,128)(2,1)} %param.44) | copy-start | bytes 3538948
  45.8 438.8 %copy-start.9 = (pred[4,384]{1,0:T(4,128)(4,1)S(1)}, pred[4,384]{1,0:T(4,128)(4,1)}, u32[]{:S(2)}) copy-start(pred[4,384]{1,0:T(4,128)(4,1)} %iota_compare_fusion) | copy-start | bytes 4612
  146.0 230.1 %collective-permute-start.5 = (bf16[54,1,12,64,128]{4,3,2,0,1:T(8,128)(2,1)}, bf16[54,1,12,64,128]{4,3,2,0,1:T(8,128)(2,1)}, u32[]{:S(2)}, u32[]{:S(2)}) collective-permute-start(bf16[54,1,12,64,128]{4,3,2,0,1:T(8,128)(2,1)} %bitcast.1130), channel_id=1, source_target_pairs={{16,0},{0,16},{17,1},{1,17},{18,2},{2,18},{19,3},{3,19},{20,4},{4,... | collective-permute-start | bytes 31850504 | tf_op jit(solution)/shard_map/cond/branch_5_fun/ppermute | solution.py:13
  512.0 105.9 %all-reduce.35.cloned.1.call-start = ((), (), s32[]{:S(2)}) async-start(), calls=%async_computation.5 | async-start | bytes 3538944 | tf_op jit(solution)/shard_map/cond/branch_5_fun/psum | solution.py:104
  685.1 100.4 %all-reduce.51.cloned.1.call-start = ((), (), s32[]{:S(2)}) async-start(), calls=%async_computation.13 | async-start | bytes 3538944 | tf_op jit(solution)/shard_map/cond/branch_5_fun/psum | solution.py:104
  853.1 100.5 %all-reduce.67.cloned.1.call-start = ((), (), s32[]{:S(2)}) async-start(), calls=%async_computation.21 | async-start | bytes 3538944 | tf_op jit(solution)/shard_map/cond/branch_5_fun/psum | solution.py:104
  971.2 1.4 copy-start.3
  972.6 17.8 %copy-start.1 = (bf16[1,4,384,384]{3,2,1,0:T(8,128)(2,1)S(1)}, bf16[1,4,384,384]{3,2,1,0:T(8,128)(2,1)}, u32[]{:S(2)}) copy-start(bf16[1,4,384,384]{3,2,1,0:T(8,128)(2,1)} %param.47) | copy-start | bytes 3538948
Sparse Core Ops, SparseCore 0:
  519.3 98.4 all-reduce.34
  692.5 93.0 all-reduce.50
  860.5 93.0 all-reduce.66
where the time goes:
time: 1010 us; the launch traced here: 997 us
  waiting for transfers between devices  513 us (51%)
  local copies, waits for them, and re-layouts  264 us (26%)
  matrix products  82.1 us (8%)
  loops' own time  62 us (6%)
  other arithmetic  34 us (3%)
  between operations  26.7 us (3%)
  blocking collectives  12.6 us (1%)
    psum x3, waiting for transfers between devices, run(): summed = lax.psum(pack(partial, order, size, 1), 'ops')  283 us
    ppermute x2, waiting for transfers between devices, from_behind(): return lax.ppermute(block, axis, route)  230 us
    reshape x8, local copies, waits for them, and re-layouts, tiled(): array.reshape(array.shape[:-2] + (block_size // ROW_TILE, ROW_TILE, block...  91.4 us
    scatter x7, local copies, waits for them, and re-layouts, unpack(): return room.at[where].set(packed, mode='drop').reshape(like.shape)  63.3 us
    dot_general x3, matrix products, on_device(): jnp.einsum('ckqad,ckqed->cqae', products, right_ops, preferred_element_ty...  61.1 us
    cond x2, local copies, waits for them, and re-layouts, chain_move(): lax.switch(choice, [branch(s) for s in classes], env, send_order, recv_or...  56.5 us
    another operation x3, loops' own time, ops_sum(): lax.switch(choice, [branch(s) for s in classes], partial, order, count)  37.9 us
    another operation x1, loops' own time, chain_move(): lax.switch(choice, [branch(s) for s in classes], env, send_order, recv_or...  24.1 us
  transfers between devices with their start and end apart: 5, of which 4 were waited for; matrix products, arithmetic and copies ran while one was open for 3% of the time, Pallas kernels for 0%

commit v1 on v0

--- a/solution.py
+++ b/solution.py
@@ -101,7 +101,7 @@
     def branch(size):
 
         def run(partial, order, count):
-            summed = lax.psum(pack(partial, order, size, 1), "ops")
+            summed = jnp.sum(lax.all_gather(pack(partial, order, size, 1), "ops"), axis=0)
             return unpack(summed, order, count, size, partial, 1)
 
         return run

time: 1010 us -> 1360 us (1.35)
  waiting for transfers between devices: 513 us -> 816 us
  other arithmetic: 34 us -> 57.7 us
  starting transfers between devices: 3.13 us -> 18.2 us
    all_gather x0 -> x3, waiting for transfers between devices: none -> 587 us  [run(): lax.all_gather(pack(partial, order, size, 1), 'ops')]
    psum x3 -> x0, waiting for transfers between devices: 283 us -> none  [run(): summed = lax.psum(pack(partial, order, size, 1), 'ops')]
    reduce_sum x0 -> x3, other arithmetic: none -> 24.2 us  [run(): jnp.sum(lax.all_gather(pack(partial, order, size, 1), 'ops'), axis=0)]
    all_gather x0 -> x3, starting transfers between devices: none -> 15.2 us  [run(): lax.all_gather(pack(partial, order, size, 1), 'ops')]
  transfers between devices with their start and end apart: 5 -> 5, of which waited for: 4 -> 4; matrix products, arithmetic and copies ran while one was open for 3% -> 2% of each run, Pallas kernels for 0% -> 0%
where the time goes in v1:
time: 1360 us; the launch traced here: 1350 us
  waiting for transfers between devices  816 us (60%)
  local copies, waits for them, and re-layouts  264 us (19%)
  matrix products  82.1 us (6%)
  loops' own time  72.3 us (5%)
  other arithmetic  57.7 us (4%)
  between operations  25.9 us (2%)
  starting transfers between devices  18.2 us (1%)
    all_gather x3, waiting for transfers between devices, run(): lax.all_gather(pack(partial, order, size, 1), 'ops')  587 us
    ppermute x2, waiting for transfers between devices, from_behind(): return lax.ppermute(block, axis, route)  230 us
    reshape x8, local copies, waits for them, and re-layouts, tiled(): array.reshape(array.shape[:-2] + (block_size // ROW_TILE, ROW_TILE, block...  91.4 us
    scatter x7, local copies, waits for them, and re-layouts, unpack(): return room.at[where].set(packed, mode='drop').reshape(like.shape)  63.3 us
    dot_general x3, matrix products, on_device(): jnp.einsum('ckqad,ckqed->cqae', products, right_ops, preferred_element_ty...  61.1 us
    cond x2, local copies, waits for them, and re-layouts, chain_move(): lax.switch(choice, [branch(s) for s in classes], env, send_order, recv_or...  56.5 us
    another operation x3, loops' own time, ops_sum(): lax.switch(choice, [branch(s) for s in classes], partial, order, count)  50.5 us
  transfers between devices with their start and end apart: 5, of which 4 were waited for; matrix products, arithmetic and copies ran while one was open for 2% of the time, Pallas kernels for 0%

profile of v1, /device:TPU:0, one launch (start us, length us, event | category | flops | bytes accessed | tf_op | source)
XLA Modules:
  0.0 1348.9 jit_solution(8335729926075792634)
XLA Ops:
  7.2 3.0 collective-permute-start.8
  12.2 5.2 all-gather.24
  19.7 21.1 %convert_bitcast_fusion = bf16[1,12,4,384,384]{3,4,1,2,0:T(8,128)(2,1)} fusion(bf16[1,4,384,384]{3,2,1,0:T(8,128)(2,1)S(1)} %copy-done, bf16[1,12,4,384,384]{4,3,2,1,0:T(8,128)(2,1)} %param.45), kind=kOutput, calls=%fused_computation.911 | convolution fusion | flops 10885791744 | bytes 29491200 | tf_op jit(solution)/shard_map/cqba,ckqbd->ckqad/dot_general | solution.py:147
  45.8 436.5 %conditional.4 = (bf16[12,4,384,384]{3,2,0,1:T(8,128)(2,1)}) conditional(s32[]{:T(128)} %clamp.28, (s32[]{:T(128)}, s32[72]{0:T(128)S(1)}, bf16[1,12,4,384,384]{3,4,1,2,0:T(8,128)(2,1)}, s32[72]{0:T(128)S(1)}) %tuple.124, (s32[]{:T(128)}, s32[72]{0:T(128)S(1)}, bf16[1,12,4,384,384]{3,4,1,2,0:T(8,128)(2,1)}, ...), branch_computations={%region_8.10_spmd, %region_10.12_spmd, %region_12.14_spmd, %region... | conditional | flops 6480 | bytes 254806912 | solution.py:96
  56.4 42.8 %reshape.1908 = bf16[12,4,6,64,3,128]{3,2,5,4,0,1:T(8,128)(2,1)} reshape(bf16[1,12,4,384,384]{3,4,1,2,0:T(8,128)(2,1)} %get-tuple-element.537) | data formatting | bytes 28311552 | tf_op jit(solution)/shard_map/cond/branch_5_fun/reshape | solution.py:60
  99.1 34.4 %copy.314 = bf16[12,4,6,64,3,128]{5,3,4,2,1,0:T(8,128)(2,1)} copy(bf16[12,4,6,64,3,128]{3,2,5,4,0,1:T(8,128)(2,1)} %reshape.1908) | data formatting | bytes 28311552 | tf_op jit(solution)/shard_map/cond/branch_5_fun/reshape | solution.py:60
  133.6 12.7 gather_fusion.5
  146.9 229.5 %collective-permute-done.5 = bf16[54,1,12,64,128]{4,3,2,0,1:T(8,128)(2,1)} collective-permute-done((bf16[54,1,12,64,128]{4,3,2,0,1:T(8,128)(2,1)}, bf16[54,1,12,64,128]{4,3,2,0,1:T(8,128)(2,1)}, u32[]{:S(2)}, u32[]{:S(2)}) %collective-permute-start.5) | collective-permute-done | bytes 10616864 | tf_op jit(solution)/shard_map/cond/branch_5_fun/ppermute | solution.py:13
  376.5 8.6 broadcast.2387
  385.1 29.5 %scatter_fusion.5 = bf16[12,4,6,64,3,128]{5,3,4,2,1,0:T(8,128)(2,1)} fusion(bf16[12,4,6,64,3,128]{5,3,4,2,1,0:T(8,128)(2,1)} %broadcast.2387, s32[54]{0:T(128)S(1)} %fusion.77, bf16[54,12,64,128]{3,2,1,0:T(8,128)(2,1)} %bitcast.35), kind=kCustom, calls=%fused_computation.37 | custom fusion | bytes 31851144 | tf_op jit(solution)/shard_map/cond/branch_5_fun/scatter | solution.py:76
  414.6 20.5 %copy.450 = bf16[12,4,6,64,3,128]{5,4,3,2,0,1:T(4,128)(2,1)} copy(bf16[12,4,6,64,3,128]{5,3,4,2,1,0:T(8,128)(2,1)} %scatter_fusion.5) | data formatting | bytes 28311552 | tf_op jit(solution)/shard_map/cond | solution.py:96
  435.1 35.9 %reshape.1916 = bf16[12,4,384,384]{3,2,0,1:T(8,128)(2,1)} reshape(bf16[12,4,6,64,3,128]{5,4,3,2,0,1:T(4,128)(2,1)} %copy.450) | data formatting | bytes 28311552 | tf_op jit(solution)/shard_map/cond | solution.py:96
  482.3 20.6 %fusion.415 = f32[1,4,384,384]{3,2,1,0:T(8,128)S(1)} fusion(bf16[12,4,384,384]{3,2,0,1:T(8,128)(2,1)} %get-tuple-element.547, bf16[1,4,384,384]{3,2,1,0:T(8,128)(2,1)S(1)} %copy-done.2, pred[4,384]{1,0:T(4,128)(4,1)S(1)} %copy-done.6, bf16[1,12,4,384,384]{4,3,2,1,0:T(8,128)(2,1)} %param.46), kind=kOutput, calls=%fused_computation.956 | convolution fusion | flops 10881073152 | bytes 31852032 | tf_op jit(solution)/shard_map/ckqad,ckqed->cqae/dot_general | solution.py:161
  503.0 255.0 %conditional.5 = (f32[1,4,384,384]{3,2,1,0:T(8,128)S(1)}) conditional(s32[]{:T(128)} %clamp.28, (s32[]{:T(128)}, s32[72]{0:T(128)S(1)}, f32[1,4,384,384]{3,2,1,0:T(8,128)S(1)}) %tuple.125, (s32[]{:T(128)}, s32[72]{0:T(128)S(1)}, f32[1,4,384,384]{3,2,1,0:T(8,128)S(1)}) %tuple.125, (s32[]{:T(128)}, s32[72]{0:T(128)S(1)}, ...), branch_computations={%region_24.27_spmd, %region_27.30_spmd, %region_30.33_spmd, %regio... | conditional | flops 4134816 | bytes 117968312 | solution.py:109
  508.1 4.9 all-gather.60.cloned.1.call-start
  513.1 2.5 reshape.1001
  520.9 200.2 %all-gather.60.cloned.1.call-done = f32[432,64,128]{2,1,0:T(8,128)} async-done(((f32[54,64,128]{2,1,0:T(8,128)}), f32[432,64,128]{2,1,0:T(8,128)}) %all-gather.60.cloned.1.call-update) | async-done | bytes 14155792 | tf_op jit(solution)/shard_map/cond/branch_5_fun/all_gather | solution.py:104
  721.0 8.1 reduce.49
  729.4 7.9 scatter_fusion.13
  737.2 3.4 copy.331
  740.6 3.8 reshape.836
  764.1 2.7 stack.71
  767.5 2.5 psum.21
  775.2 20.2 %fusion.420 = f32[1,4,384,384]{3,2,1,0:T(8,128)S(1)} fusion(bf16[12,4,384,384]{3,2,0,1:T(8,128)(2,1)} %get-tuple-element.547, bf16[1,4,384,384]{3,2,1,0:T(8,128)(2,1)S(1)} %fusion.406, bf16[1,12,4,384,384]{4,3,2,1,0:T(8,128)(2,1)} %param.46), kind=kOutput, calls=%fused_computation.957 | convolution fusion | flops 10878713856 | bytes 31850496 | tf_op jit(solution)/shard_map/ckqad,ckqed->cqae/dot_general | solution.py:161
  795.4 248.4 %conditional.6 = (f32[1,4,384,384]{3,2,1,0:T(8,128)S(1)}) conditional(s32[]{:T(128)} %clamp.28, (s32[]{:T(128)}, s32[72]{0:T(128)S(1)}, f32[1,4,384,384]{3,2,1,0:T(8,128)S(1)}) %tuple.126, (s32[]{:T(128)}, s32[72]{0:T(128)S(1)}, f32[1,4,384,384]{3,2,1,0:T(8,128)S(1)}) %tuple.126, (s32[]{:T(128)}, s32[72]{0:T(128)S(1)}, ...), branch_computations={%region_57.60_spmd, %region_60.63_spmd, %region_63.66_spmd, %regio... | conditional | flops 4134816 | bytes 117968312 | solution.py:109
  800.3 5.0 all-gather.76.cloned.1.call-start
  805.3 2.5 reshape.1065
  813.1 193.3 %all-gather.76.cloned.1.call-done = f32[432,64,128]{2,1,0:T(8,128)} async-done(((f32[54,64,128]{2,1,0:T(8,128)}), f32[432,64,128]{2,1,0:T(8,128)}) %all-gather.76.cloned.1.call-update) | async-done | bytes 14155792 | tf_op jit(solution)/shard_map/cond/branch_5_fun/all_gather | solution.py:104
  1006.4 8.1 reduce.57
  1014.8 7.9 scatter_fusion.21
  1022.6 3.4 copy.347
  1026.1 3.8 reshape.852
  1048.9 2.5 stack.77
  1052.1 2.5 psum.22
  1057.8 2.4 fusion.459
  1060.2 20.3 %fusion.425 = f32[1,4,384,384]{3,2,1,0:T(8,128)S(1)} fusion(bf16[12,4,384,384]{3,2,0,1:T(8,128)(2,1)} %get-tuple-element.547, bf16[1,4,384,384]{3,2,1,0:T(8,128)(2,1)} %get-tuple-element.616, bf16[1,12,4,384,384]{4,3,2,1,0:T(8,128)(2,1)} %param.46), kind=kOutput, calls=%fused_computation.958 | convolution fusion | flops 10878713856 | bytes 31850496 | tf_op jit(solution)/shard_map/ckqad,ckqed->cqae/dot_general | solution.py:161
  1080.4 242.7 %conditional.7 = (f32[1,4,384,384]{3,2,1,0:T(8,128)S(1)}) conditional(s32[]{:T(128)} %clamp.28, (s32[]{:T(128)}, s32[72]{0:T(128)S(1)}, f32[1,4,384,384]{3,2,1,0:T(8,128)S(1)}) %tuple.127, (s32[]{:T(128)}, s32[72]{0:T(128)S(1)}, f32[1,4,384,384]{3,2,1,0:T(8,128)S(1)}) %tuple.127, (s32[]{:T(128)}, s32[72]{0:T(128)S(1)}, ...), branch_computations={%region_89.92_spmd, %region_92.95_spmd, %region_95.98_spmd, %regio... | conditional | flops 4134816 | bytes 117968312 | solution.py:109
  1085.4 5.3 all-gather.92.cloned.1.call-start
  1090.7 2.5 reshape.1129
  1098.4 193.3 %all-gather.92.cloned.1.call-done = f32[432,64,128]{2,1,0:T(8,128)} async-done(((f32[54,64,128]{2,1,0:T(8,128)}), f32[432,64,128]{2,1,0:T(8,128)}) %all-gather.92.cloned.1.call-update) | async-done | bytes 14155792 | tf_op jit(solution)/shard_map/cond/branch_5_fun/all_gather | solution.py:104
  1291.7 8.1 reduce.65
  1300.1 7.9 scatter_fusion.29
  1308.0 3.4 copy.363
  1311.4 3.8 reshape.868
  1324.5 3.2 multiply_reduce_fusion.2
  1329.7 2.5 multiply_reduce_fusion
  1332.1 2.6 stack.83
  1335.4 2.5 psum.23
  (91 shorter events, 44.0 us)
Async XLA Ops:
  7.2 12.5 copy-start
  7.2 37.0 %collective-permute-start.8 = (s32[1,4]{1,0:T(1,128)}, s32[1,4]{1,0:T(1,128)S(1)}, u32[]{:S(2)}, u32[]{:S(2)}) collective-permute-start(s32[1,4]{1,0:T(1,128)} %param.48), channel_id=1, source_target_pairs={{16,0},{0,16},{17,1},{1,17},{18,2},{2,18},{19,3},{3,19},{20,4},{4,... | collective-permute-start | bytes 56 | tf_op jit(solution)/shard_map/ppermute | solution.py:13
  19.7 21.9 %copy-start.8 = (s32[8]{0:T(128)S(1)}, s32[8]{0:T(128)}, u32[]{:S(2)}) copy-start(s32[8]{0:T(128)} %constant.1772.clone) | copy-start | bytes 100
  19.7 23.8 %copy-start.7 = (s32[2]{0:T(128)S(1)}, s32[2]{0:T(128)}, u32[]{:S(2)}) copy-start(s32[2]{0:T(128)} %constant.1763.clone.1) | copy-start | bytes 28
  45.8 436.5 %copy-start.2 = (bf16[1,4,384,384]{3,2,1,0:T(8,128)(2,1)S(1)}, bf16[1,4,384,384]{3,2,1,0:T(8,128)(2,1)}, u32[]{:S(2)}) copy-start(bf16[1,4,384,384]{3,2,1,0:T(8,128)(2,1)} %param.44) | copy-start | bytes 3538948
  45.8 436.5 %copy-start.6 = (pred[4,384]{1,0:T(4,128)(4,1)S(1)}, pred[4,384]{1,0:T(4,128)(4,1)}, u32[]{:S(2)}) copy-start(pred[4,384]{1,0:T(4,128)(4,1)} %iota_compare_fusion) | copy-start | bytes 4612
  146.3 230.2 %collective-permute-start.5 = (bf16[54,1,12,64,128]{4,3,2,0,1:T(8,128)(2,1)}, bf16[54,1,12,64,128]{4,3,2,0,1:T(8,128)(2,1)}, u32[]{:S(2)}, u32[]{:S(2)}) collective-permute-start(bf16[54,1,12,64,128]{4,3,2,0,1:T(8,128)(2,1)} %bitcast.1118), channel_id=1, source_target_pairs={{16,0},{0,16},{17,1},{1,17},{18,2},{2,18},{19,3},{3,19},{20,4},{4,... | collective-permute-start | bytes 31850504 | tf_op jit(solution)/shard_map/cond/branch_5_fun/ppermute | solution.py:13
  508.1 212.9 %all-gather.60.cloned.1.call-start = ((), (), s32[]{:S(2)}) async-start(), calls=%async_computation.5 | async-start | bytes 15925248 | tf_op jit(solution)/shard_map/cond/branch_5_fun/all_gather | solution.py:104
  800.3 206.1 %all-gather.76.cloned.1.call-start = ((), (), s32[]{:S(2)}) async-start(), calls=%async_computation.13 | async-start | bytes 15925248 | tf_op jit(solution)/shard_map/cond/branch_5_fun/all_gather | solution.py:104
  1085.4 206.4 %all-gather.92.cloned.1.call-start = ((), (), s32[]{:S(2)}) async-start(), calls=%async_computation.21 | async-start | bytes 15925248 | tf_op jit(solution)/shard_map/cond/branch_5_fun/all_gather | solution.py:104
  1323.1 1.4 copy-start.3
  1324.5 17.6 %copy-start.1 = (bf16[1,4,384,384]{3,2,1,0:T(8,128)(2,1)S(1)}, bf16[1,4,384,384]{3,2,1,0:T(8,128)(2,1)}, u32[]{:S(2)}) copy-start(bf16[1,4,384,384]{3,2,1,0:T(8,128)(2,1)} %param.47) | copy-start | bytes 3538948
Sparse Core Ops, SparseCore 0:
  520.4 200.5 all-gather.59
  812.6 193.7 all-gather.75
  1097.9 193.7 all-gather.91
